TPU v7x, 256 devices: a whole 4x4x8 slice. The times are simulated.
256 devices in a mesh: scen: 64 (over y, x, z_hi, core), trade: 4 (over z_lo).
Axes of the slice: x: 4, y: 4, z: 8 (z_hi: 2, z_lo: 4; z = z_hi * 4 + z_lo), core: 2. Of those that a mesh axis runs over, the one named last changes fastest.
Arguments:
- payoffs: float32 [12, 12, 12, 4, 8192], P(None, None, None, 'trade', 'scen'), may hold values from -4 to 4
- sweep_counts: int32 [4, 8192], P('trade', 'scen'), may hold values from 1 to 6
- netting_map: int32 [4, 8192], P('trade'), may hold values from 0 to 511
- type_lengths: int32 [8], replicated, may hold values from 1 to 8192, 32768 in all
- type_diffusion: float32 [8], replicated, may hold values from 0.02 to 0.15
- type_discount: float32 [8], replicated, may hold values from 0.01 to 0.12
- factors: float32 [3, 8192], P(None, 'scen'), may hold values from -1 to 1
Outputs:
- exposures: float32 [8192, 512], P('scen', 'trade')
- allocation: float32 [4, 8192], P('trade', 'scen')
All inputs are finite; a program needn't handle non-finite values.
Results may differ from a plain program's by a relative error of at most 0.0055.
Values may be sent and summed in bfloat16 or wider, within the bound.
No kernel may reach another device: no remote copies, remote signals or barrier semaphores. Data moves between devices by JAX's collectives and lax.ppermute only.
A program may use at most 128 MiB of HBM per device.

v0:
```python
import jax
import jax.numpy as jnp
from jax import lax
from jax.sharding import PartitionSpec as P

GRID = 12
NETS = 512
TYPES = 8
MAX_SWEEPS = 6


def cheb_matrix():
    intervals = GRID - 1
    order_index = jnp.arange(GRID, dtype=jnp.float32)
    end_weights = jnp.where((order_index == 0) | (order_index == intervals), 0.5, 1.0).astype(
        jnp.float32
    )
    angles = jnp.pi * order_index[:, None] * order_index[None, :] / intervals
    return 2.0 / intervals * end_weights[:, None] * end_weights[None, :] * jnp.cos(angles)


def cheb_basis(factors):
    factor_basis = []
    for column in range(3):
        point = factors[column]
        recurrence = [jnp.ones_like(point), point]
        for degree in range(2, GRID):
            recurrence.append(2.0 * point * recurrence[-1] - recurrence[-2])
        factor_basis.append(jnp.stack(recurrence[:GRID], 0))
    product = factor_basis[0][:, None, None, :] * factor_basis[1][None, :, None, :]
    product = product * factor_basis[2][None, None, :, :]
    return product.reshape(GRID * GRID * GRID, -1).astype(jnp.bfloat16)


def price(grid_values, counts, trade_index, type_lengths, type_diffusion, type_discount):
    type_ends = jnp.cumsum(type_lengths)
    type_ids = jnp.sum((trade_index[:, None] >= type_ends[None, :]).astype(jnp.int32), axis=1)
    type_hot = (type_ids[:, None] == jnp.arange(TYPES, dtype=jnp.int32)[None, :]).astype(
        jnp.float32
    )
    diffusion = jnp.sum(type_hot * type_diffusion[None, :], axis=1)
    discount = jnp.sum(type_hot * type_discount[None, :], axis=1)

    def smooth_step(degree, field):
        padded = jnp.pad(field, ((1, 1), (1, 1), (1, 1), (0, 0)))
        beside = padded[2:, 1:-1, 1:-1] + padded[:-2, 1:-1, 1:-1]
        beside = beside + padded[1:-1, 2:, 1:-1] + padded[1:-1, :-2, 1:-1]
        beside = beside + padded[1:-1, 1:-1, 2:] + padded[1:-1, 1:-1, :-2]
        updated = field + diffusion * (beside - 6.0 * field) - discount * field
        return jnp.where(degree < counts, updated, field)

    field = lax.fori_loop(0, MAX_SWEEPS, smooth_step, grid_values)
    matrix = cheb_matrix()
    field = jnp.einsum("ai,ijlp->ajlp", matrix, field, precision=lax.Precision.HIGHEST)
    field = jnp.einsum("bj,ajlp->ablp", matrix, field, precision=lax.Precision.HIGHEST)
    field = jnp.einsum("cl,ablp->abcp", matrix, field, precision=lax.Precision.HIGHEST)
    return field.reshape(GRID * GRID * GRID, -1).astype(jnp.bfloat16)


def shards(
    payoffs, sweep_counts, netting_map, type_lengths, type_diffusion, type_discount, factors
):
    trades_here = payoffs.shape[4]
    scen_index = lax.axis_index("scen")
    group_index = lax.axis_index("trade")
    block_size = trades_here * lax.axis_size("scen")
    first_trade = group_index * block_size + scen_index * trades_here
    trade_index = first_trade + jnp.arange(trades_here, dtype=jnp.int32)
    coef_local = price(
        payoffs[:, :, :, 0, :],
        sweep_counts[0],
        trade_index,
        type_lengths,
        type_diffusion,
        type_discount,
    )
    group_ids = netting_map[0]
    classes = jnp.arange(NETS, dtype=jnp.int32)
    scen_rows = factors.shape[1]
    scen_total = scen_rows * lax.axis_size("scen")
    basis_rows = cheb_basis(factors)
    values = lax.dot_general(
        basis_rows,
        lax.all_gather(coef_local, "scen", axis=1, tiled=True),
        (((0,), (0,)), ((), ())),
        preferred_element_type=jnp.float32,
    )
    set_hot = (group_ids[:, None] == classes[None, :]).astype(jnp.float32)
    partial_value = jnp.dot(values, set_hot, precision=lax.Precision.HIGHEST)
    totals = lax.psum_scatter(partial_value, "trade", scatter_dimension=1, tiled=True)
    exposures = jnp.maximum(totals, 0.0)
    every_set = lax.all_gather(exposures, "trade", axis=1, tiled=True)
    weight_rows = jnp.dot(every_set, set_hot.T, precision=lax.Precision.HIGHEST)
    alloc_terms = jnp.sum(values * weight_rows, axis=0) / scen_total
    allocation = lax.psum_scatter(alloc_terms, "scen", scatter_dimension=0, tiled=True)
    return (exposures, allocation.reshape(1, trades_here))


def solution(mesh):
    return jax.shard_map(
        shards,
        mesh=mesh,
        in_specs=(
            P(None, None, None, "trade", "scen"),
            P("trade", "scen"),
            P("trade", None),
            P(),
            P(),
            P(),
            P(None, "scen"),
        ),
        out_specs=(P("scen", "trade"), P("trade", "scen")),
        check_vma=False,
    )
```

profile of v0, /device:TPU:32, one launch (start us, length us, event | category | flops | bytes accessed | tf_op | source)
XLA Modules:
  0.0 805.9 jit_solution(13713044818506615753)
XLA Ops:
  7.3 1.3 copy.21
  9.0 5.0 while.15
  9.1 0.7 fusion.45
  9.9 0.7 fusion.45
  10.8 0.7 fusion.45
  11.6 0.7 fusion.45
  12.5 0.7 fusion.45
  13.3 0.7 fusion.45
  14.0 1.6 fusion.19
  15.6 1.7 convolution_bitcast_fusion
  17.3 1.5 fusion.16
  18.9 0.9 convert_element_type.33
  19.8 0.2 reduce-scatter.2.cloned.1.call-start
  20.5 308.7 %all-gather.2.cloned.1.call-done = bf16[1728,8192]{1,0:T(8,128)(2,1)} async-done(((bf16[1728,128]{1,0:T(8,128)(2,1)}), bf16[1728,8192]{1,0:T(8,128)(2,1)}) %all-gather.2.cloned.1.call-update) | async-done | bytes 28311568 | tf_op jit(solution)/shard_map/all_gather | solution.py:84
  329.2 11.2 %fusion.39 = f32[128,8192]{1,0:T(8,128)S(1)} fusion(bf16[1728,128]{1,0:T(8,128)(2,1)S(1)} %convert_element_type.29, bf16[1728,8192]{1,0:T(8,128)(2,1)} %all-gather.2.cloned.1.call-done), kind=kOutput, calls=%fused_computation.97 | convolution fusion | flops 3623878656 | bytes 32948224 | tf_op jit(solution)/shard_map/dot_general | solution.py:82
  340.4 1.9 copy-done
  342.3 6.6 fusion.11
  349.0 0.6 dynamic-slice
  350.2 17.3 %reduce-scatter.2.cloned.1.call-done = f32[128,128]{1,0:T(8,128)} async-done(((f32[128,512]{1,0:T(8,128)}), f32[128,128]{1,0:T(8,128)}) %reduce-scatter.2.cloned.1.call-update) | async-done | bytes 65552 | tf_op jit(solution)/shard_map/reduce_scatter | solution.py:90
  367.5 0.8 broadcast_maximum_fusion
  368.4 14.5 %all_gather.7 = f32[128,512]{1,0:T(8,128)S(1)} all-gather(f32[128,128]{1,0:T(8,128)S(1)} %broadcast_maximum_fusion), channel_id=1, replica_groups=mesh['scen'=64,'trade'=4] {'trade'}, dimensions={1}, use_global_device_ids=true | all-gather | bytes 327680 | tf_op jit(solution)/shard_map/all_gather | solution.py:92
  382.8 11.0 %fusion.15 = f32[8192]{0:T(1024)S(1)} fusion(f32[128,8192]{1,0:T(8,128)} %copy-done, f32[128,512]{1,0:T(8,128)S(1)} %all_gather.7, s32[8192]{0:T(1024)S(1)} %bitcast.29), kind=kOutput, calls=%fused_computation.23 | convolution fusion | flops 6448734208 | bytes 4521984 | tf_op jit(solution)/shard_map/dot_general | solution.py:93
  393.9 404.6 %all-reduce.1 = f32[8192]{0:T(1024)S(1)} all-reduce(f32[8192]{0:T(1024)S(1)} %broadcast_multiply_fusion.1), channel_id=3, replica_groups=mesh['scen'=64,'trade'=4] {'scen'}, use_global_device_ids=true, to_apply=%region_8.9.clone | all-reduce | flops 8192 | bytes 65536
  798.5 0.6 dynamic-slice_bitcast_fusion
  (49 shorter events, 1.7 us)
Async XLA Ops:
  7.2 1.4 copy-start.6
  7.2 1.7 copy-start.4
  7.2 1.7 copy-start.3
  7.2 1.8 copy-start.7
  7.2 322.0 %all-gather.2.cloned.1.call-start = ((), (), s32[]{:S(2)}) async-start(), calls=%async_computation.1 | async-start | bytes 28753920 | tf_op jit(solution)/shard_map/all_gather | solution.py:84
  18.8 1.1 copy-start.2
  19.8 347.8 %reduce-scatter.2.cloned.1.call-start = ((), (), s32[]{:S(2)}) async-start(), calls=%async_computation.2 | async-start | bytes 327680 | tf_op jit(solution)/shard_map/reduce_scatter | solution.py:90
  20.5 321.8 %copy-start.5 = (s32[1,8192]{1,0:T(1,128)S(1)}, s32[1,8192]{1,0:T(1,128)}, u32[]{:S(2)}) copy-start(s32[1,8192]{1,0:T(1,128)} %param.11) | copy-start | bytes 98308
  340.4 1.9 copy-start
  342.3 6.6 copy-start.8
  368.4 25.5 %copy-start.1 = (f32[128,128]{1,0:T(8,128)}, f32[128,128]{1,0:T(8,128)S(1)}, u32[]{:S(2)}) copy-start(f32[128,128]{1,0:T(8,128)S(1)} %broadcast_maximum_fusion) | copy-start | bytes 196612
Sparse Core Ops, SparseCore 0:
  19.9 309.3 all-gather.1
  349.1 18.4 reduce-scatter.1
where the time goes:
time: 806 us
  blocking collectives  419 us (52%)
  waiting for transfers between devices  326 us (40%)
  matrix products  33.6 us (4%)
  between operations  14.9 us (2%)
    unnamed x1, blocking collectives  405 us
    all_gather x1, waiting for transfers between devices, shards(): lax.all_gather(coef_local, 'scen', axis=1, tiled=True)  309 us
    reduce_scatter x1, waiting for transfers between devices, shards(): lax.psum_scatter(partial_value, 'trade', scatter_dimension=1, tiled=True)  17.3 us
  transfers between devices with their start and end apart: 2, of which 2 were waited for; matrix products, arithmetic and copies ran while one was open for 0% of the time, Pallas kernels for 0%

commit v1 on v0

--- a/solution.py
+++ b/solution.py
@@ -81,7 +81,15 @@
     basis_rows = cheb_basis(factors)
     values = lax.dot_general(
         basis_rows,
-        lax.all_gather(coef_local, "scen", axis=1, tiled=True),
+        jnp.concatenate(
+            lax.all_to_all(
+                jnp.stack([coef_local for _ in range(lax.axis_size("scen"))]),
+                split_axis=0,
+                axis_name="scen",
+                concat_axis=0,
+            ),
+            axis=1,
+        ),
         (((0,), (0,)), ((), ())),
         preferred_element_type=jnp.float32,
     )

time: 806 us -> 1210 us (1.50)
  waiting for transfers between devices: 326 us -> 703 us
  starting transfers between devices: 0.26 us -> 14.2 us
    all_to_all x0 -> x1, waiting for transfers between devices: none -> 608 us  [shards(): lax.all_to_all(jnp.stack([coef_local for _ in range(lax.axis_size('scen')...]
    all_gather x1 -> x0, waiting for transfers between devices: 309 us -> none  [shards(): lax.all_gather(coef_local, 'scen', axis=1, tiled=True)]
    reduce_scatter x1, waiting for transfers between devices: 17.3 us -> 94.8 us  [shards(): lax.psum_scatter(partial_value, 'trade', scatter_dimension=1, tiled=True)]
    all_to_all x0 -> x1, starting transfers between devices: none -> 14 us  [shards(): lax.all_to_all(jnp.stack([coef_local for _ in range(lax.axis_size('scen')...]
where the time goes in v1:
time: 1210 us
  waiting for transfers between devices  703 us (58%)
  blocking collectives  419 us (35%)
  matrix products  33.6 us (3%)
  between operations  14.9 us (1%)
  local copies, waits for them, and re-layouts  14.8 us (1%)
  starting transfers between devices  14.2 us (1%)
    all_to_all x1, waiting for transfers between devices, shards(): lax.all_to_all(jnp.stack([coef_local for _ in range(lax.axis_size('scen')...  608 us
    unnamed x1, blocking collectives  405 us
    reduce_scatter x1, waiting for transfers between devices, shards(): lax.psum_scatter(partial_value, 'trade', scatter_dimension=1, tiled=True)  94.8 us
  transfers between devices with their start and end apart: 2, of which 2 were waited for; matrix products, arithmetic and copies ran while one was open for 0% of the time, Pallas kernels for 0%

profile of v1, /device:TPU:32, one launch (start us, length us, event | category | flops | bytes accessed | tf_op | source)
XLA Modules:
  0.0 1205.3 jit_solution(17413640995366753927)
XLA Ops:
  7.3 1.3 copy.31
  8.9 4.7 while.15
  9.0 0.7 fusion.47
  9.8 0.7 fusion.47
  10.6 0.7 fusion.47
  11.4 0.7 fusion.47
  12.2 0.7 fusion.47
  12.9 0.7 fusion.47
  13.6 1.6 fusion.22
  15.2 1.7 convolution_bitcast_fusion
  17.0 1.5 fusion.19
  18.6 9.6 stack.11
  28.2 14.0 %all-to-all-start = ((bf16[64,1728,128]{2,1,0:T(8,128)(2,1)}), bf16[64,1728,128]{2,1,0:T(8,128)(2,1)}, u32[]{:S(2)}, u32[]{:S(2)}) async-start(bf16[64,1728,128]{2,1,0:T(8,128)(2,1)} %stack.11), calls=%async_computation | async-start | bytes 56623104 | tf_op jit(solution)/shard_map/all_to_all | solution.py:85
  43.0 608.1 %all-to-all-done = bf16[64,1728,128]{2,1,0:T(8,128)(2,1)} async-done(((bf16[64,1728,128]{2,1,0:T(8,128)(2,1)}), bf16[64,1728,128]{2,1,0:T(8,128)(2,1)}, u32[]{:S(2)}, u32[]{:S(2)}) %all-to-all-start) | async-done | bytes 28311584 | tf_op jit(solution)/shard_map/all_to_all | solution.py:85
  651.0 11.2 fusion.10
  662.2 1.9 copy-done.8
  664.1 6.6 fusion.14
  670.8 0.6 dynamic-slice
  672.0 94.8 %reduce-scatter.2.cloned.1.call-done = f32[128,128]{1,0:T(8,128)} async-done(((f32[128,512]{1,0:T(8,128)}), f32[128,128]{1,0:T(8,128)}) %reduce-scatter.2.cloned.1.call-update) | async-done | bytes 65552 | tf_op jit(solution)/shard_map/reduce_scatter | solution.py:98
  766.8 0.8 broadcast_maximum_fusion
  767.6 14.4 %all_gather.3 = f32[128,512]{1,0:T(8,128)S(1)} all-gather(f32[128,128]{1,0:T(8,128)S(1)} %broadcast_maximum_fusion), channel_id=1, replica_groups=mesh['scen'=64,'trade'=4] {'trade'}, dimensions={1}, use_global_device_ids=true | all-gather | bytes 327680 | tf_op jit(solution)/shard_map/all_gather | solution.py:100
  782.0 11.0 fusion.18
  793.1 404.8 %all-reduce.1 = f32[8192]{0:T(1024)S(1)} all-reduce(f32[8192]{0:T(1024)S(1)} %broadcast_multiply_fusion.1), channel_id=3, replica_groups=mesh['scen'=64,'trade'=4] {'scen'}, use_global_device_ids=true, to_apply=%region_8.9.clone | all-reduce | flops 8192 | bytes 65536
  1197.9 0.6 dynamic-slice_bitcast_fusion
  (49 shorter events, 1.7 us)
Async XLA Ops:
  7.2 1.4 copy-start.5
  7.2 1.6 copy-start.3
  7.2 1.6 copy-start.2
  7.2 1.7 copy-start.6
  28.2 14.3 %copy-start.1 = (f32[3,128]{1,0:T(4,128)S(1)}, f32[3,128]{1,0:T(4,128)}, u32[]{:S(2)}) copy-start(f32[3,128]{1,0:T(4,128)} %param.15) | copy-start | bytes 4612
  28.2 622.8 %all-to-all-start = ((bf16[64,1728,128]{2,1,0:T(8,128)(2,1)}), bf16[64,1728,128]{2,1,0:T(8,128)(2,1)}, u32[]{:S(2)}, u32[]{:S(2)}) async-start(bf16[64,1728,128]{2,1,0:T(8,128)(2,1)} %stack.11), calls=%async_computation | async-start | bytes 56623104 | tf_op jit(solution)/shard_map/all_to_all | solution.py:85
  42.2 724.6 %reduce-scatter.2.cloned.1.call-start = ((), (), s32[]{:S(2)}) async-start(), calls=%async_computation.2 | async-start | bytes 327680 | tf_op jit(solution)/shard_map/reduce_scatter | solution.py:98
  42.9 621.2 %copy-start.4 = (s32[1,8192]{1,0:T(1,128)S(1)}, s32[1,8192]{1,0:T(1,128)}, u32[]{:S(2)}) copy-start(s32[1,8192]{1,0:T(1,128)} %param.11) | copy-start | bytes 98308
  662.2 1.9 copy-start.8
  664.1 6.6 copy-start.7
  767.6 25.4 %copy-start = (f32[128,128]{1,0:T(8,128)}, f32[128,128]{1,0:T(8,128)S(1)}, u32[]{:S(2)}) copy-start(f32[128,128]{1,0:T(8,128)S(1)} %broadcast_maximum_fusion) | copy-start | bytes 196612
Sparse Core Ops, SparseCore 0:
  670.9 95.8 reduce-scatter.1
